TPU v7x, 256 devices: a whole 4x4x8 slice. The times are simulated.
256 devices in a mesh: row: 8 (over x, core), col: 32 (over y, z).
Axes of the slice: x: 4, y: 4, z: 8, core: 2. Of those that a mesh axis runs over, the one named last changes fastest.
Arguments:
- tokens: bfloat16 [512, 8192], P('col', 'row'), may hold values from -6 to 6
- cotangent: bfloat16 [512, 8192], P('col', 'row'), may hold values from -6 to 6
- gate_weight: bfloat16 [8192, 28672], P('row', 'col'), may hold values from -0.09375 to 0.09375
- up_weight: bfloat16 [8192, 28672], P('row', 'col'), may hold values from -0.09375 to 0.09375
- down_weight: bfloat16 [28672, 8192], P('col', 'row'), may hold values from -0.046875 to 0.046875
- block_mask: int32 [3, 64, 224], P(None, 'row', 'col'), may hold values 0 or 1
Outputs:
- layer_out: bfloat16 [512, 8192], P('col', 'row')
- token_grad: bfloat16 [512, 8192], P('col', 'row')
- gate_grad: bfloat16 [8192, 28672], P('row', 'col')
- up_grad: bfloat16 [8192, 28672], P('row', 'col')
- down_grad: bfloat16 [28672, 8192], P('col', 'row')
All inputs are finite; a program needn't handle non-finite values. No bound on the sum of `block_mask` on one device may be relied on, other than what follows from the above.
Results may differ from a plain program's by a relative error of at most 0.025.
Values may be sent and summed in bfloat16 or wider, within the bound.
No kernel may reach another device: no remote copies, remote signals or barrier semaphores. Data moves between devices by JAX's collectives and lax.ppermute only.
A program may use at most 64 MiB of HBM per device.

v0:
```python
import jax
import jax.numpy as jnp
from jax import lax
from jax.sharding import PartitionSpec as P


def masked(weight, mask):
    rows, cols = mask.shape
    shaped = weight.reshape(rows, weight.shape[0] // rows, cols, weight.shape[1] // cols)
    return (shaped * mask.astype(weight.dtype)[:, None, :, None]).reshape(weight.shape)


def product(left, weight):
    return jnp.dot(left, weight, preferred_element_type=jnp.float32)


def product_t(left, weight):
    return lax.dot_general(
        left, weight, (((1,), (1,)), ((), ())), preferred_element_type=jnp.float32
    )


def contract_rows(left, right):
    return lax.dot_general(
        left, right, (((0,), (0,)), ((), ())), preferred_element_type=jnp.float32
    )


def gather_rows(local, axis, size):
    sent = jnp.broadcast_to(local[None], (size,) + local.shape)
    got = lax.all_to_all(sent, axis, 0, 0, tiled=False)
    return got.reshape((size * local.shape[0],) + local.shape[1:])


def reduce_rows(partial, axis, size):
    chunks = partial.astype(jnp.bfloat16).reshape(
        (size, partial.shape[0] // size) + partial.shape[1:]
    )
    got = lax.all_to_all(chunks, axis, 0, 0, tiled=False)
    return got.astype(jnp.float32).sum(axis=0)


def shards(tokens, cotangent, gate_weight, up_weight, down_weight, block_mask):
    n_row = lax.axis_size("row")
    n_col = lax.axis_size("col")
    masked_gate = masked(gate_weight, block_mask[0])
    masked_up = masked(up_weight, block_mask[1])
    masked_down = masked(down_weight, block_mask[2].T)
    feat = tokens.shape[1]
    panel = gather_rows(tokens, "col", n_col)
    grad_panel = gather_rows(cotangent, "col", n_col)
    total_rows = panel.shape[0]
    width = masked_gate.shape[1]
    fwd = reduce_rows(
        jnp.concatenate(
            [
                product(panel, masked_gate).astype(jnp.bfloat16),
                product(panel, masked_up).astype(jnp.bfloat16),
            ],
            axis=1,
        ),
        "row",
        n_row,
    )
    gate = fwd[:, :width]
    up = fwd[:, width:]
    sigma = jax.nn.sigmoid(gate)
    act = (gate * sigma * up).astype(jnp.bfloat16)
    act_full = lax.all_gather(act, "row", axis=0, tiled=True)
    layer_out = reduce_rows(product(act_full, masked_down), "col", n_col).astype(jnp.bfloat16)
    dact = reduce_rows(product_t(grad_panel, masked_down), "row", n_row)
    dgate = (dact * up * sigma * (1.0 + gate * (1.0 - sigma))).astype(jnp.bfloat16)
    dup = (dact * gate * sigma).astype(jnp.bfloat16)
    full = lax.all_gather(jnp.concatenate([dgate, dup], axis=1), "row", axis=0, tiled=True)
    dgate_full = full[:, :width]
    dup_full = full[:, width:]
    token_grad = reduce_rows(
        product_t(dgate_full, masked_gate) + product_t(dup_full, masked_up), "col", n_col
    ).astype(jnp.bfloat16)
    scale = total_rows ** (-0.5)
    gate_grad = masked(contract_rows(panel, dgate_full) * scale, block_mask[0]).astype(jnp.bfloat16)
    up_grad = masked(contract_rows(panel, dup_full) * scale, block_mask[1]).astype(jnp.bfloat16)
    down_grad = masked(contract_rows(act_full, grad_panel) * scale, block_mask[2].T).astype(
        jnp.bfloat16
    )
    return (layer_out, token_grad, gate_grad, up_grad, down_grad)


def solution(mesh):
    in_specs = (
        P("col", "row"),
        P("col", "row"),
        P("row", "col"),
        P("row", "col"),
        P("col", "row"),
        P(None, "row", "col"),
    )
    out_specs = (
        P("col", "row"),
        P("col", "row"),
        P("row", "col"),
        P("row", "col"),
        P("col", "row"),
    )
    return jax.shard_map(shards, mesh=mesh, in_specs=in_specs, out_specs=out_specs, check_vma=False)
```

profile of v0, /device:TPU:32, one launch (start us, length us, event | category | flops | bytes accessed | tf_op | source)
XLA Modules:
  0.0 223.7 jit_solution(11346078941495549265)
XLA Ops:
  7.2 0.9 broadcast_in_dim.5
  8.1 39.7 %all_to_all.30 = bf16[32,16,1024]{2,1,0:T(8,128)(2,1)S(1)} all-to-all(bf16[32,16,1024]{2,1,0:T(8,128)(2,1)S(1)} %broadcast_in_dim.5), channel_id=1, replica_groups=mesh['row'=8,'col'=32] {'col'}, dimensions={0} | all-to-all | bytes 2097152 | tf_op jit(solution)/shard_map/all_to_all | solution.py:31
  47.7 1.1 broadcast_in_dim.4
  48.8 5.3 %all-to-all-start = ((bf16[32,16,1024]{2,1,0:T(8,128)(2,1)}), bf16[32,16,1024]{2,1,0:T(8,128)(2,1)}, u32[]{:S(2)}, u32[]{:S(2)}) async-start(bf16[32,16,1024]{2,1,0:T(8,128)(2,1)} %broadcast_in_dim.4), calls=%async_computation | async-start | bytes 2097152 | tf_op jit(solution)/shard_map/all_to_all | solution.py:31
  54.2 2.4 %copy.20 = bf16[1024,896]{0,1:T(8,128)(2,1)} copy(bf16[1024,896]{1,0:T(8,128)(2,1)S(1)} %copy-done.2) | data formatting | bytes 3670016 | tf_op args[3]
  56.7 3.8 %copy.18 = bf16[1024,896]{0,1:T(8,128)(2,1)} copy(bf16[1024,896]{1,0:T(8,128)(2,1)} %param.8) | data formatting | bytes 3670016 | tf_op args[2]
  60.6 0.3 mul.114
  60.9 1.2 copy-done.8
  62.1 0.2 copy-done.13
  62.3 2.3 %convolution_convert_fusion.1 = bf16[896,512]{0,1:T(8,128)(2,1)} fusion(bf16[512,1024]{1,0:T(8,128)(2,1)S(1)} %bitcast.85, bf16[896,1024]{1,0:T(8,128)(2,1)S(1)} %copy-done.13, bf16[112,8,8,128]{3,2,1,0:T(8,128)(2,1)S(1)} %bitcast.91), kind=kOutput, calls=%fused_computation.14 | convolution fusion | flops 940900352 | bytes 5636096 | tf_op jit(solution)/shard_map/dot_general | solution.py:18
  64.5 17.6 %all-to-all-done = bf16[32,16,1024]{2,1,0:T(8,128)(2,1)} async-done(((bf16[32,16,1024]{2,1,0:T(8,128)(2,1)}), bf16[32,16,1024]{2,1,0:T(8,128)(2,1)}, u32[]{:S(2)}, u32[]{:S(2)}) %all-to-all-start) | async-done | bytes 1048608 | tf_op jit(solution)/shard_map/all_to_all | solution.py:31
  82.2 4.4 %all-to-all-start.4 = ((bf16[8,64,896]{2,1,0:T(8,128)(2,1)}), bf16[8,64,896]{2,1,0:T(8,128)(2,1)}, u32[]{:S(2)}, u32[]{:S(2)}) async-start(bf16[8,64,896]{2,1,0:T(8,128)(2,1)} %bitcast.97), calls=%async_computation.4 | async-start | bytes 1835008 | tf_op jit(solution)/shard_map/all_to_all | solution.py:39
  86.6 0.3 mul.109
  86.9 1.2 copy-done.6
  88.1 2.4 %fusion.4 = bf16[512,896]{0,1:T(8,128)(2,1)S(1)} fusion(bf16[512,1024]{1,0:T(8,128)(2,1)} %bitcast.1, bf16[1024,896]{0,1:T(8,128)(2,1)S(1)} %copy-done.3, bf16[112,8,8,128]{3,2,1,0:T(8,128)(2,1)S(1)} %bitcast.89), kind=kOutput, calls=%fused_computation.18 | convolution fusion | flops 940900352 | bytes 5636096 | tf_op jit(solution)/shard_map/dot_general | solution.py:14
  90.5 0.3 mul.106
  90.9 1.7 copy-done.5
  92.6 2.4 %fusion.3 = bf16[512,896]{0,1:T(8,128)(2,1)S(1)} fusion(bf16[512,1024]{1,0:T(8,128)(2,1)} %bitcast.1, bf16[1024,896]{0,1:T(8,128)(2,1)S(1)} %copy-done.5, bf16[112,8,8,128]{3,2,1,0:T(8,128)(2,1)S(1)} %bitcast.93), kind=kOutput, calls=%fused_computation.17 | convolution fusion | flops 940900352 | bytes 5636096 | tf_op jit(solution)/shard_map/dot_general | solution.py:14
  95.1 2.4 %copy.21 = bf16[512,1792]{1,0:T(8,128)(2,1)} copy(bf16[512,1792]{0,1:T(8,128)(2,1)S(1)} %pad_maximum_fusion) | data formatting | bytes 3670016 | tf_op jit(solution)/shard_map/concatenate | solution.py:55
  97.5 3.8 %all-to-all-done.4 = bf16[8,64,896]{2,1,0:T(8,128)(2,1)} async-done(((bf16[8,64,896]{2,1,0:T(8,128)(2,1)}), bf16[8,64,896]{2,1,0:T(8,128)(2,1)}, u32[]{:S(2)}, u32[]{:S(2)}) %all-to-all-start.4) | async-done | bytes 917536 | tf_op jit(solution)/shard_map/all_to_all | solution.py:39
  101.2 3.6 %all-to-all-start.1 = ((bf16[8,64,1792]{2,1,0:T(8,128)(2,1)}), bf16[8,64,1792]{2,1,0:T(8,128)(2,1)S(1)}, u32[]{:S(2)}, u32[]{:S(2)}) async-start(bf16[8,64,1792]{2,1,0:T(8,128)(2,1)} %bitcast.5), calls=%async_computation.1 | async-start | bytes 3670016 | tf_op jit(solution)/shard_map/all_to_all | solution.py:39
  104.9 1.3 convert_reduce_fusion.1
  106.2 22.9 %all-to-all-done.1 = bf16[8,64,1792]{2,1,0:T(8,128)(2,1)S(1)} async-done(((bf16[8,64,1792]{2,1,0:T(8,128)(2,1)}), bf16[8,64,1792]{2,1,0:T(8,128)(2,1)S(1)}, u32[]{:S(2)}, u32[]{:S(2)}) %all-to-all-start.1) | async-done | bytes 1835040 | tf_op jit(solution)/shard_map/all_to_all | solution.py:39
  129.1 0.2 convert_reduce_fusion
  129.4 0.2 multiply_convert_fusion.1
  129.5 0.7 pad_maximum_fusion.1
  130.3 14.7 %all_gather.6 = bf16[512,896]{1,0:T(8,128)(2,1)S(1)} all-gather(bf16[64,896]{1,0:T(8,128)(2,1)S(1)} %get-tuple-element.17), channel_id=1, replica_groups=mesh['row'=8,'col'=32] {'row'}, dimensions={0}, use_global_device_ids=true | all-gather | bytes 1032192 | tf_op jit(solution)/shard_map/all_gather | solution.py:69
  145.0 4.1 %convolution_convert_fusion = bf16[512,1024]{1,0:T(8,128)(2,1)} fusion(bf16[512,896]{1,0:T(8,128)(2,1)S(1)} %all_gather.6, bf16[896,1024]{1,0:T(8,128)(2,1)} %param.10, bf16[112,8,8,128]{3,2,1,0:T(8,128)(2,1)S(1)} %bitcast.92), kind=kOutput, calls=%fused_computation.13 | convolution fusion | flops 940965888 | bytes 5636096 | tf_op jit(solution)/shard_map/dot_general | solution.py:14
  149.2 4.3 %all-to-all-start.2 = ((bf16[32,16,1024]{2,1,0:T(8,128)(2,1)}), bf16[32,16,1024]{2,1,0:T(8,128)(2,1)S(1)}, u32[]{:S(2)}, u32[]{:S(2)}) async-start(bf16[32,16,1024]{2,1,0:T(8,128)(2,1)} %bitcast.96), calls=%async_computation.2 | async-start | bytes 2097152 | tf_op jit(solution)/shard_map/all_to_all | solution.py:39
  153.5 3.7 %fusion.8 = f32[512,1024]{1,0:T(8,128)S(1)} fusion(bf16[512,1792]{1,0:T(8,128)(2,1)} %all-gather.2.cloned.1.call-done, bf16[1024,896]{0,1:T(8,128)(2,1)} %copy.18, bf16[112,8,8,128]{3,2,1,0:T(8,128)(2,1)} %bitcast.94), kind=kOutput, calls=%fused_computation.22 | convolution fusion | flops 940441600 | bytes 6684672 | tf_op jit(solution)/shard_map/dot_general | solution.py:18
  157.3 0.2 copy-done.14
  157.5 2.2 %add_convert_fusion = bf16[512,1024]{1,0:T(8,128)(2,1)} fusion(f32[512,1024]{1,0:T(8,128)S(1)} %fusion.8, bf16[512,1792]{1,0:T(8,128)(2,1)S(1)} %copy-done.14, bf16[1024,896]{0,1:T(8,128)(2,1)S(1)} %copy-done.4, bf16[112,8,8,128]{3,2,1,0:T(8,128)(2,1)S(1)} %bitcast.90), kind=kOutput, calls=%fused_computation.7 | convolution fusion | flops 941490176 | bytes 7733248 | tf_op jit(solution)/shard_map/dot_general | solution.py:18
  159.7 22.5 %all-to-all-done.2 = bf16[32,16,1024]{2,1,0:T(8,128)(2,1)S(1)} async-done(((bf16[32,16,1024]{2,1,0:T(8,128)(2,1)}), bf16[32,16,1024]{2,1,0:T(8,128)(2,1)S(1)}, u32[]{:S(2)}, u32[]{:S(2)}) %all-to-all-start.2) | async-done | bytes 1048608 | tf_op jit(solution)/shard_map/all_to_all | solution.py:39
  182.2 5.6 %all-to-all-start.5 = ((bf16[32,16,1024]{2,1,0:T(8,128)(2,1)}), bf16[32,16,1024]{2,1,0:T(8,128)(2,1)S(1)}, u32[]{:S(2)}, u32[]{:S(2)}) async-start(bf16[32,16,1024]{2,1,0:T(8,128)(2,1)} %bitcast.95), calls=%async_computation.5 | async-start | bytes 2097152 | tf_op jit(solution)/shard_map/all_to_all | solution.py:39
  188.1 0.3 mul.134
  188.4 0.9 copy-done.1
  189.3 2.8 %fusion = bf16[896,1024]{1,0:T(8,128)(2,1)} fusion(f32[112,8,8,128]{3,2,1,0:T(8,128)S(1)} %bitcast.84, bf16[512,896]{1,0:T(8,128)(2,1)S(1)} %copy-done.1, bf16[512,1024]{1,0:T(8,128)(2,1)S(1)} %bitcast.86), kind=kOutput, calls=%fused_computation.1 | convolution fusion | flops 942276608 | bytes 7471104 | tf_op jit(solution)/shard_map/dot_general | solution.py:24
  192.1 0.8 reduce_sum.43
  192.9 0.3 mul.125
  193.2 1.2 copy-done.15
  194.4 4.0 %fusion.2 = bf16[1024,896]{0,1:T(8,128)(2,1)} fusion(f32[112,8,8,128]{3,2,1,0:T(8,128)S(1)} %bitcast.88, bf16[512,1024]{1,0:T(8,128)(2,1)} %bitcast.1, bf16[512,1792]{1,0:T(8,128)(2,1)S(1)} %copy-done.15), kind=kOutput, calls=%fused_computation.5 | convolution fusion | flops 942276608 | bytes 7471104 | tf_op jit(solution)/shard_map/dot_general | solution.py:24
  198.4 3.8 %copy.26 = bf16[1024,896]{1,0:T(8,128)(2,1)} copy(bf16[1024,896]{0,1:T(8,128)(2,1)} %fusion.2) | data formatting | bytes 3670016
  202.2 0.3 mul.130
  202.5 1.2 copy-done.16
  203.7 4.0 %fusion.1 = bf16[1024,896]{0,1:T(8,128)(2,1)} fusion(f32[112,8,8,128]{3,2,1,0:T(8,128)S(1)} %bitcast.87, bf16[512,1024]{1,0:T(8,128)(2,1)} %bitcast.1, bf16[512,1792]{1,0:T(8,128)(2,1)S(1)} %copy-done.16), kind=kOutput, calls=%fused_computation.3 | convolution fusion | flops 942276608 | bytes 7471104 | tf_op jit(solution)/shard_map/dot_general | solution.py:24
  207.7 3.8 %copy.27 = bf16[1024,896]{1,0:T(8,128)(2,1)} copy(bf16[1024,896]{0,1:T(8,128)(2,1)} %fusion.1) | data formatting | bytes 3670016
  211.5 4.6 %all-to-all-done.5 = bf16[32,16,1024]{2,1,0:T(8,128)(2,1)S(1)} async-done(((bf16[32,16,1024]{2,1,0:T(8,128)(2,1)}), bf16[32,16,1024]{2,1,0:T(8,128)(2,1)S(1)}, u32[]{:S(2)}, u32[]{:S(2)}) %all-to-all-start.5) | async-done | bytes 1048608 | tf_op jit(solution)/shard_map/all_to_all | solution.py:39
  216.1 0.8 reduce_sum.45
  (37 shorter events, 0.8 us)
Async XLA Ops:
  7.2 40.6 %copy-start.11 = (bf16[16,1024]{1,0:T(8,128)(2,1)S(1)}, bf16[16,1024]{1,0:T(8,128)(2,1)}, u32[]{:S(2)}) copy-start(bf16[16,1024]{1,0:T(8,128)(2,1)} %param.6) | copy-start | bytes 98308
  47.7 6.4 %copy-start.12 = (s32[3,8,7]{2,1,0:T(8,128)S(1)}, s32[3,8,7]{2,1,0:T(8,128)}, u32[]{:S(2)}) copy-start(s32[3,8,7]{2,1,0:T(8,128)} %param.11) | copy-start | bytes 2020
  47.7 6.5 %copy-start.2 = (bf16[1024,896]{1,0:T(8,128)(2,1)S(1)}, bf16[1024,896]{1,0:T(8,128)(2,1)}, u32[]{:S(2)}) copy-start(bf16[1024,896]{1,0:T(8,128)(2,1)} %param.9) | copy-start | bytes 5505028
  48.8 33.3 %all-to-all-start = ((bf16[32,16,1024]{2,1,0:T(8,128)(2,1)}), bf16[32,16,1024]{2,1,0:T(8,128)(2,1)}, u32[]{:S(2)}, u32[]{:S(2)}) async-start(bf16[32,16,1024]{2,1,0:T(8,128)(2,1)} %broadcast_in_dim.4), calls=%async_computation | async-start | bytes 2097152 | tf_op jit(solution)/shard_map/all_to_all | solution.py:31
  60.5 1.8 copy-start.13
  60.9 1.2 copy-start.8
  82.2 6.0 %copy-start.3 = (bf16[1024,896]{0,1:T(8,128)(2,1)S(1)}, bf16[1024,896]{0,1:T(8,128)(2,1)}, u32[]{:S(2)}) copy-start(bf16[1024,896]{0,1:T(8,128)(2,1)} %copy.20) | copy-start | bytes 5505028
  82.2 19.1 %all-to-all-start.4 = ((bf16[8,64,896]{2,1,0:T(8,128)(2,1)}), bf16[8,64,896]{2,1,0:T(8,128)(2,1)}, u32[]{:S(2)}, u32[]{:S(2)}) async-start(bf16[8,64,896]{2,1,0:T(8,128)(2,1)} %bitcast.97), calls=%async_computation.4 | async-start | bytes 1835008 | tf_op jit(solution)/shard_map/all_to_all | solution.py:39
  86.9 1.2 copy-start.6
  90.5 2.0 copy-start.5
  90.8 4.1 %copy-start.10 = (bf16[8,128,7,128]{1,0,3,2:T(8,128)(2,1)}, bf16[8,128,7,128]{1,0,3,2:T(8,128)(2,1)S(1)}, u32[]{:S(2)}) copy-start(bf16[8,128,7,128]{1,0,3,2:T(8,128)(2,1)S(1)} %mul.106) | copy-start | bytes 5505028
  101.2 27.9 %all-to-all-start.1 = ((bf16[8,64,1792]{2,1,0:T(8,128)(2,1)}), bf16[8,64,1792]{2,1,0:T(8,128)(2,1)S(1)}, u32[]{:S(2)}, u32[]{:S(2)}) async-start(bf16[8,64,1792]{2,1,0:T(8,128)(2,1)} %bitcast.5), calls=%async_computation.1 | async-start | bytes 3670016 | tf_op jit(solution)/shard_map/all_to_all | solution.py:39
  104.8 48.7 %all-gather.2.cloned.1.call-start = ((), (), s32[]{:S(2)}) async-start(), calls=%async_computation.6 | async-start | bytes 2064384 | tf_op jit(solution)/shard_map/all_gather | solution.py:74
  129.4 15.7 %copy-start.9 = (bf16[7,128,8,128]{3,2,1,0:T(8,128)(2,1)S(1)}, bf16[7,128,8,128]{3,2,1,0:T(8,128)(2,1)}, u32[]{:S(2)}) copy-start(bf16[7,128,8,128]{3,2,1,0:T(8,128)(2,1)} %copy-done.8) | copy-start | bytes 5505028
  145.0 4.1 %copy-start = (bf16[512,896]{1,0:T(8,128)(2,1)}, bf16[512,896]{1,0:T(8,128)(2,1)S(1)}, u32[]{:S(2)}) copy-start(bf16[512,896]{1,0:T(8,128)(2,1)S(1)} %all_gather.6) | copy-start | bytes 2752516
  149.2 33.0 %all-to-all-start.2 = ((bf16[32,16,1024]{2,1,0:T(8,128)(2,1)}), bf16[32,16,1024]{2,1,0:T(8,128)(2,1)S(1)}, u32[]{:S(2)}, u32[]{:S(2)}) async-start(bf16[32,16,1024]{2,1,0:T(8,128)(2,1)} %bitcast.96), calls=%async_computation.2 | async-start | bytes 2097152 | tf_op jit(solution)/shard_map/all_to_all | solution.py:39
  153.5 3.8 %copy-start.4 = (bf16[1024,896]{0,1:T(8,128)(2,1)S(1)}, bf16[1024,896]{0,1:T(8,128)(2,1)}, u32[]{:S(2)}) copy-start(bf16[1024,896]{0,1:T(8,128)(2,1)} %copy.20) | copy-start | bytes 5505028
  153.5 3.8 %copy-start.7 = (bf16[8,128,7,128]{1,0,3,2:T(8,128)(2,1)S(1)}, bf16[8,128,7,128]{1,0,3,2:T(8,128)(2,1)}, u32[]{:S(2)}) copy-start(bf16[8,128,7,128]{1,0,3,2:T(8,128)(2,1)} %copy-done.6) | copy-start | bytes 5505028
  153.5 4.0 %copy-start.14 = (bf16[512,1792]{1,0:T(8,128)(2,1)S(1)}, bf16[512,1792]{1,0:T(8,128)(2,1)}, u32[]{:S(2)}) copy-start(bf16[512,1792]{1,0:T(8,128)(2,1)} %all-gather.2.cloned.1.call-done) | copy-start | bytes 5505028
  182.2 33.9 %all-to-all-start.5 = ((bf16[32,16,1024]{2,1,0:T(8,128)(2,1)}), bf16[32,16,1024]{2,1,0:T(8,128)(2,1)S(1)}, u32[]{:S(2)}, u32[]{:S(2)}) async-start(bf16[32,16,1024]{2,1,0:T(8,128)(2,1)} %bitcast.95), calls=%async_computation.5 | async-start | bytes 2097152 | tf_op jit(solution)/shard_map/all_to_all | solution.py:39
  188.1 1.2 copy-start.1
  192.9 1.5 copy-start.15
  202.2 1.5 copy-start.16
Sparse Core Ops, SparseCore 0:
  130.4 22.2 all-gather.1
where the time goes:
time: 225 us; the launch traced here: 224 us
  waiting for transfers between devices  71.3 us (32%)
  blocking collectives  54.4 us (24%)
  local copies, waits for them, and re-layouts  28.3 us (13%)
  matrix products  28 us (12%)
  starting transfers between devices  23.3 us (10%)
  between operations  14.3 us (6%)
  other arithmetic  4.1 us (2%)
    all_to_all x4, waiting for transfers between devices, reduce_rows(): got = lax.all_to_all(chunks, axis, 0, 0, tiled=False)  53.7 us
    all_to_all x1, blocking collectives, gather_rows(): got = lax.all_to_all(sent, axis, 0, 0, tiled=False)  39.7 us
    unnamed x38, local copies, waits for them, and re-layouts  21.6 us
    all_to_all x4, starting transfers between devices, reduce_rows(): got = lax.all_to_all(chunks, axis, 0, 0, tiled=False)  18 us
    all_to_all x1, waiting for transfers between devices, gather_rows(): got = lax.all_to_all(sent, axis, 0, 0, tiled=False)  17.6 us
    all_gather x1, blocking collectives, shards(): act_full = lax.all_gather(act, 'row', axis=0, tiled=True)  14.7 us
    dot_general x3, matrix products, contract_rows(): lax.dot_general(left, right, (((0,), (0,)), ((), ())), preferred_element_...  10.9 us
    dot_general x3, matrix products, product(): return jnp.dot(left, weight, preferred_element_type=jnp.float32)  8.88 us
  transfers between devices with their start and end apart: 6, of which 5 were waited for; matrix products, arithmetic and copies ran while one was open for 22% of the time, Pallas kernels for 0%

commit v1 on v0

--- a/solution.py
+++ b/solution.py
@@ -66,7 +66,23 @@
     up = fwd[:, width:]
     sigma = jax.nn.sigmoid(gate)
     act = (gate * sigma * up).astype(jnp.bfloat16)
-    act_full = lax.all_gather(act, "row", axis=0, tiled=True)
+    block_last = lax.axis_index("row")
+    step_out = lax.axis_size("row")
+    res, b_now, aux = (step_out, block_last, act.shape[0])
+    items = [(src_i, (src_i + 1) % res) for src_i in range(res)]
+    buffers = [(src_i, (src_i - 1) % res) for src_i in range(res)]
+    act_full = jnp.zeros((*act.shape[:0], res * aux, *act.shape[1:]), act.dtype)
+    inter = carry_in = act
+    local_next = res // 2
+    act_full = lax.dynamic_update_slice_in_dim(act_full, act, b_now * aux, axis=0)
+    for j in range(1, local_next + 1):
+        inter = lax.ppermute(inter, axis_name="row", perm=items)
+        act_full = lax.dynamic_update_slice_in_dim(act_full, inter, (b_now - j) % res * aux, axis=0)
+        if j < res - local_next:
+            carry_in = lax.ppermute(carry_in, perm=buffers, axis_name="row")
+            act_full = lax.dynamic_update_slice_in_dim(
+                act_full, carry_in, (b_now + j) % res * aux, axis=0
+            )
     layer_out = reduce_rows(product(act_full, masked_down), "col", n_col).astype(jnp.bfloat16)
     dact = reduce_rows(product_t(grad_panel, masked_down), "row", n_row)
     dgate = (dact * up * sigma * (1.0 + gate * (1.0 - sigma))).astype(jnp.bfloat16)

time: 225 us -> 232 us (1.031)
  the two profiles are of different devices: /device:TPU:32 before, /device:TPU:6 now
where the time goes in v1:
time: 232 us; the launch traced here: 231 us
  waiting for transfers between devices  78 us (34%)
  blocking collectives  39.9 us (17%)
  starting transfers between devices  36.3 us (16%)
  local copies, waits for them, and re-layouts  29 us (12%)
  matrix products  28.5 us (12%)
  between operations  14.3 us (6%)
  other arithmetic  4.86 us (2%)
    all_to_all x4, waiting for transfers between devices, reduce_rows(): got = lax.all_to_all(chunks, axis, 0, 0, tiled=False)  47.2 us
    all_to_all x1, blocking collectives, gather_rows(): got = lax.all_to_all(sent, axis, 0, 0, tiled=False)  39.9 us
    all_to_all x4, starting transfers between devices, reduce_rows(): got = lax.all_to_all(chunks, axis, 0, 0, tiled=False)  23.9 us
    unnamed x38, local copies, waits for them, and re-layouts  22.1 us
    all_to_all x1, waiting for transfers between devices, gather_rows(): got = lax.all_to_all(sent, axis, 0, 0, tiled=False)  18 us
    ppermute x4, waiting for transfers between devices, shards(): inter = lax.ppermute(inter, axis_name='row', perm=items)  12.8 us
    dot_general x3, matrix products, contract_rows(): lax.dot_general(left, right, (((0,), (0,)), ((), ())), preferred_element_...  10.9 us
    dot_general x3, matrix products, product(): return jnp.dot(left, weight, preferred_element_type=jnp.float32)  9.39 us
  transfers between devices with their start and end apart: 13, of which 9 were waited for; matrix products, arithmetic and copies ran while one was open for 22% of the time, Pallas kernels for 0%

profile of v1, /device:TPU:6, one launch (start us, length us, event | category | flops | bytes accessed | tf_op | source)
XLA Modules:
  0.0 231.0 jit_solution(17216714909335383678)
XLA Ops:
  7.2 0.9 broadcast_in_dim.8
  8.1 39.9 %all_to_all.30 = bf16[32,16,1024]{2,1,0:T(8,128)(2,1)S(1)} all-to-all(bf16[32,16,1024]{2,1,0:T(8,128)(2,1)S(1)} %broadcast_in_dim.8), channel_id=1, replica_groups=mesh['row'=8,'col'=32] {'col'}, dimensions={0} | all-to-all | bytes 2097152 | tf_op jit(solution)/shard_map/all_to_all | solution.py:31
  48.0 1.1 broadcast_in_dim.7
  49.1 5.2 %all-to-all-start = ((bf16[32,16,1024]{2,1,0:T(8,128)(2,1)}), bf16[32,16,1024]{2,1,0:T(8,128)(2,1)}, u32[]{:S(2)}, u32[]{:S(2)}) async-start(bf16[32,16,1024]{2,1,0:T(8,128)(2,1)} %broadcast_in_dim.7), calls=%async_computation | async-start | bytes 2097152 | tf_op jit(solution)/shard_map/all_to_all | solution.py:31
  54.3 2.4 %copy.20 = bf16[1024,896]{0,1:T(8,128)(2,1)} copy(bf16[1024,896]{1,0:T(8,128)(2,1)S(1)} %copy-done.2) | data formatting | bytes 3670016 | tf_op args[3]
  56.8 3.8 %copy.18 = bf16[1024,896]{0,1:T(8,128)(2,1)} copy(bf16[1024,896]{1,0:T(8,128)(2,1)} %param.8) | data formatting | bytes 3670016 | tf_op args[2]
  60.8 0.3 mul.146
  61.1 1.2 copy-done.8
  62.4 2.2 convolution_convert_fusion.1
  64.6 18.0 %all-to-all-done = bf16[32,16,1024]{2,1,0:T(8,128)(2,1)} async-done(((bf16[32,16,1024]{2,1,0:T(8,128)(2,1)}), bf16[32,16,1024]{2,1,0:T(8,128)(2,1)}, u32[]{:S(2)}, u32[]{:S(2)}) %all-to-all-start) | async-done | bytes 1048608 | tf_op jit(solution)/shard_map/all_to_all | solution.py:31
  82.5 4.9 %all-to-all-start.4 = ((bf16[8,64,896]{2,1,0:T(8,128)(2,1)}), bf16[8,64,896]{2,1,0:T(8,128)(2,1)}, u32[]{:S(2)}, u32[]{:S(2)}) async-start(bf16[8,64,896]{2,1,0:T(8,128)(2,1)} %bitcast.97), calls=%async_computation.4 | async-start | bytes 1835008 | tf_op jit(solution)/shard_map/all_to_all | solution.py:39
  87.8 1.2 copy-done.6
  89.0 2.4 %fusion.4 = bf16[512,896]{0,1:T(8,128)(2,1)S(1)} fusion(bf16[512,1024]{1,0:T(8,128)(2,1)} %bitcast.1, bf16[1024,896]{0,1:T(8,128)(2,1)S(1)} %copy-done.3, bf16[112,8,8,128]{3,2,1,0:T(8,128)(2,1)S(1)} %bitcast.89), kind=kOutput, calls=%fused_computation.18 | convolution fusion | flops 940900352 | bytes 5636096 | tf_op jit(solution)/shard_map/dot_general | solution.py:14
  91.4 0.3 mul.130
  91.7 1.7 copy-done.5
  93.4 2.4 %fusion.3 = bf16[512,896]{0,1:T(8,128)(2,1)S(1)} fusion(bf16[512,1024]{1,0:T(8,128)(2,1)} %bitcast.1, bf16[1024,896]{0,1:T(8,128)(2,1)S(1)} %copy-done.5, bf16[112,8,8,128]{3,2,1,0:T(8,128)(2,1)S(1)} %bitcast.93), kind=kOutput, calls=%fused_computation.17 | convolution fusion | flops 940900352 | bytes 5636096 | tf_op jit(solution)/shard_map/dot_general | solution.py:14
  95.9 2.4 %copy.21 = bf16[512,1792]{1,0:T(8,128)(2,1)} copy(bf16[512,1792]{0,1:T(8,128)(2,1)S(1)} %pad_maximum_fusion) | data formatting | bytes 3670016 | tf_op jit(solution)/shard_map/concatenate | solution.py:55
  98.3 1.7 all-to-all-done.4
  100.0 5.6 %all-to-all-start.1 = ((bf16[8,64,1792]{2,1,0:T(8,128)(2,1)}), bf16[8,64,1792]{2,1,0:T(8,128)(2,1)S(1)}, u32[]{:S(2)}, u32[]{:S(2)}) async-start(bf16[8,64,1792]{2,1,0:T(8,128)(2,1)} %bitcast.5), calls=%async_computation.1 | async-start | bytes 3670016 | tf_op jit(solution)/shard_map/all_to_all | solution.py:39
  105.6 2.0 convert_reduce_fusion.1
  107.7 20.2 %all-to-all-done.1 = bf16[8,64,1792]{2,1,0:T(8,128)(2,1)S(1)} async-done(((bf16[8,64,1792]{2,1,0:T(8,128)(2,1)}), bf16[8,64,1792]{2,1,0:T(8,128)(2,1)S(1)}, u32[]{:S(2)}, u32[]{:S(2)}) %all-to-all-start.1) | async-done | bytes 1835040 | tf_op jit(solution)/shard_map/all_to_all | solution.py:39
  128.1 0.7 copy-done.10
  129.0 0.7 pad_maximum_fusion.1
  129.9 1.7 collective-permute-start.1
  131.6 2.5 %collective-permute-done = bf16[64,896]{1,0:T(8,128)(2,1)S(1)} collective-permute-done((bf16[64,896]{1,0:T(8,128)(2,1)S(1)}, bf16[64,896]{1,0:T(8,128)(2,1)S(1)}, u32[]{:S(2)}, u32[]{:S(2)}) %collective-permute-start) | collective-permute-done | bytes 114720 | tf_op jit(solution)/shard_map/ppermute | solution.py:79
  134.1 1.7 collective-permute-start.3
  135.9 2.4 %collective-permute-done.2 = bf16[64,896]{1,0:T(8,128)(2,1)S(1)} collective-permute-done((bf16[64,896]{1,0:T(8,128)(2,1)S(1)}, bf16[64,896]{1,0:T(8,128)(2,1)S(1)}, u32[]{:S(2)}, u32[]{:S(2)}) %collective-permute-start.2) | collective-permute-done | bytes 114720 | tf_op jit(solution)/shard_map/ppermute | solution.py:79
  138.3 1.7 collective-permute-start.4
  140.1 4.8 %collective-permute-done.4 = bf16[64,896]{1,0:T(8,128)(2,1)S(1)} collective-permute-done((bf16[64,896]{1,0:T(8,128)(2,1)S(1)}, bf16[64,896]{1,0:T(8,128)(2,1)S(1)}, u32[]{:S(2)}, u32[]{:S(2)}) %collective-permute-start.4) | collective-permute-done | bytes 114720 | tf_op jit(solution)/shard_map/ppermute | solution.py:79
  144.9 1.9 collective-permute-start.6
  146.9 3.2 %collective-permute-done.6 = bf16[64,896]{1,0:T(8,128)(2,1)S(1)} collective-permute-done((bf16[64,896]{1,0:T(8,128)(2,1)S(1)}, bf16[64,896]{1,0:T(8,128)(2,1)S(1)}, u32[]{:S(2)}, u32[]{:S(2)}) %collective-permute-start.6) | collective-permute-done | bytes 114720 | tf_op jit(solution)/shard_map/ppermute | solution.py:79
  150.1 4.6 %convolution_convert_fusion = bf16[512,1024]{1,0:T(8,128)(2,1)} fusion(bf16[512,896]{1,0:T(8,128)(2,1)S(1)} %constant_dynamic-update-slice_fusion, bf16[896,1024]{1,0:T(8,128)(2,1)} %param.10, bf16[112,8,8,128]{3,2,1,0:T(8,128)(2,1)} %bitcast.92), kind=kOutput, calls=%fused_computation.13 | convolution fusion | flops 940965888 | bytes 5636096 | tf_op jit(solution)/shard_map/dot_general | solution.py:14
  154.7 5.0 %all-to-all-start.2 = ((bf16[32,16,1024]{2,1,0:T(8,128)(2,1)}), bf16[32,16,1024]{2,1,0:T(8,128)(2,1)S(1)}, u32[]{:S(2)}, u32[]{:S(2)}) async-start(bf16[32,16,1024]{2,1,0:T(8,128)(2,1)} %bitcast.96), calls=%async_computation.2 | async-start | bytes 2097152 | tf_op jit(solution)/shard_map/all_to_all | solution.py:39
  159.8 3.7 %fusion.8 = f32[512,1024]{1,0:T(8,128)S(1)} fusion(bf16[512,1792]{1,0:T(8,128)(2,1)} %all-gather.2.cloned.1.call-done, bf16[1024,896]{0,1:T(8,128)(2,1)} %copy.18, bf16[112,8,8,128]{3,2,1,0:T(8,128)(2,1)} %bitcast.94), kind=kOutput, calls=%fused_computation.22 | convolution fusion | flops 940441600 | bytes 6684672 | tf_op jit(solution)/shard_map/dot_general | solution.py:18
  163.7 2.2 add_convert_fusion
  166.0 19.7 %all-to-all-done.2 = bf16[32,16,1024]{2,1,0:T(8,128)(2,1)S(1)} async-done(((bf16[32,16,1024]{2,1,0:T(8,128)(2,1)}), bf16[32,16,1024]{2,1,0:T(8,128)(2,1)S(1)}, u32[]{:S(2)}, u32[]{:S(2)}) %all-to-all-start.2) | async-done | bytes 1048608 | tf_op jit(solution)/shard_map/all_to_all | solution.py:39
  185.6 8.4 %all-to-all-start.5 = ((bf16[32,16,1024]{2,1,0:T(8,128)(2,1)}), bf16[32,16,1024]{2,1,0:T(8,128)(2,1)S(1)}, u32[]{:S(2)}, u32[]{:S(2)}) async-start(bf16[32,16,1024]{2,1,0:T(8,128)(2,1)} %bitcast.95), calls=%async_computation.5 | async-start | bytes 2097152 | tf_op jit(solution)/shard_map/all_to_all | solution.py:39
  194.6 0.9 copy-done.1
  195.5 2.8 %fusion = bf16[896,1024]{1,0:T(8,128)(2,1)} fusion(f32[112,8,8,128]{3,2,1,0:T(8,128)S(1)} %bitcast.84, bf16[512,896]{1,0:T(8,128)(2,1)S(1)} %copy-done.1, bf16[512,1024]{1,0:T(8,128)(2,1)S(1)} %bitcast.86), kind=kOutput, calls=%fused_computation.1 | convolution fusion | flops 942276608 | bytes 7471104 | tf_op jit(solution)/shard_map/dot_general | solution.py:24
  198.3 0.8 reduce_sum.43
  199.4 1.2 copy-done.15
  200.6 4.0 %fusion.2 = bf16[1024,896]{0,1:T(8,128)(2,1)} fusion(f32[112,8,8,128]{3,2,1,0:T(8,128)S(1)} %bitcast.88, bf16[512,1024]{1,0:T(8,128)(2,1)} %bitcast.1, bf16[512,1792]{1,0:T(8,128)(2,1)S(1)} %copy-done.15), kind=kOutput, calls=%fused_computation.5 | convolution fusion | flops 942276608 | bytes 7471104 | tf_op jit(solution)/shard_map/dot_general | solution.py:24
  204.6 3.8 %copy.26 = bf16[1024,896]{1,0:T(8,128)(2,1)} copy(bf16[1024,896]{0,1:T(8,128)(2,1)} %fusion.2) | data formatting | bytes 3670016
  208.7 1.2 copy-done.16
  209.9 4.1 %fusion.1 = bf16[1024,896]{0,1:T(8,128)(2,1)} fusion(f32[112,8,8,128]{3,2,1,0:T(8,128)S(1)} %bitcast.87, bf16[512,1024]{1,0:T(8,128)(2,1)} %bitcast.1, bf16[512,1792]{1,0:T(8,128)(2,1)S(1)} %copy-done.16), kind=kOutput, calls=%fused_computation.3 | convolution fusion | flops 942276608 | bytes 7471104 | tf_op jit(solution)/shard_map/dot_general | solution.py:24
  214.0 3.8 %copy.27 = bf16[1024,896]{1,0:T(8,128)(2,1)} copy(bf16[1024,896]{0,1:T(8,128)(2,1)} %fusion.1) | data formatting | bytes 3670016
  217.8 5.6 %all-to-all-done.5 = bf16[32,16,1024]{2,1,0:T(8,128)(2,1)S(1)} async-done(((bf16[32,16,1024]{2,1,0:T(8,128)(2,1)}), bf16[32,16,1024]{2,1,0:T(8,128)(2,1)S(1)}, u32[]{:S(2)}, u32[]{:S(2)}) %all-to-all-start.5) | async-done | bytes 1048608 | tf_op jit(solution)/shard_map/all_to_all | solution.py:39
  223.4 0.8 reduce_sum.45
  (59 shorter events, 2.8 us)
Async XLA Ops:
  7.2 40.8 %copy-start.11 = (bf16[16,1024]{1,0:T(8,128)(2,1)S(1)}, bf16[16,1024]{1,0:T(8,128)(2,1)}, u32[]{:S(2)}) copy-start(bf16[16,1024]{1,0:T(8,128)(2,1)} %param.6) | copy-start | bytes 98308
  48.0 6.3 %copy-start.2 = (bf16[1024,896]{1,0:T(8,128)(2,1)S(1)}, bf16[1024,896]{1,0:T(8,128)(2,1)}, u32[]{:S(2)}) copy-start(bf16[1024,896]{1,0:T(8,128)(2,1)} %param.9) | copy-start | bytes 5505028
  49.1 33.5 %all-to-all-start = ((bf16[32,16,1024]{2,1,0:T(8,128)(2,1)}), bf16[32,16,1024]{2,1,0:T(8,128)(2,1)}, u32[]{:S(2)}, u32[]{:S(2)}) async-start(bf16[32,16,1024]{2,1,0:T(8,128)(2,1)} %broadcast_in_dim.7), calls=%async_computation | async-start | bytes 2097152 | tf_op jit(solution)/shard_map/all_to_all | solution.py:31
  54.3 2.4 %copy-start.12 = (s32[3,8,7]{2,1,0:T(8,128)S(1)}, s32[3,8,7]{2,1,0:T(8,128)}, u32[]{:S(2)}) copy-start(s32[3,8,7]{2,1,0:T(8,128)} %param.11) | copy-start | bytes 2020
  60.6 1.8 copy-start.13
  61.1 1.3 copy-start.8
  82.5 6.4 %copy-start.3 = (bf16[1024,896]{0,1:T(8,128)(2,1)S(1)}, bf16[1024,896]{0,1:T(8,128)(2,1)}, u32[]{:S(2)}) copy-start(bf16[1024,896]{0,1:T(8,128)(2,1)} %copy.20) | copy-start | bytes 5505028
  82.5 17.5 %all-to-all-start.4 = ((bf16[8,64,896]{2,1,0:T(8,128)(2,1)}), bf16[8,64,896]{2,1,0:T(8,128)(2,1)}, u32[]{:S(2)}, u32[]{:S(2)}) async-start(bf16[8,64,896]{2,1,0:T(8,128)(2,1)} %bitcast.97), calls=%async_computation.4 | async-start | bytes 1835008 | tf_op jit(solution)/shard_map/all_to_all | solution.py:39
  87.8 1.2 copy-start.6
  91.4 2.0 copy-start.5
  91.7 4.1 %copy-start.9 = (bf16[8,128,7,128]{1,0,3,2:T(8,128)(2,1)}, bf16[8,128,7,128]{1,0,3,2:T(8,128)(2,1)S(1)}, u32[]{:S(2)}) copy-start(bf16[8,128,7,128]{1,0,3,2:T(8,128)(2,1)S(1)} %mul.130) | copy-start | bytes 5505028
  100.0 27.9 %all-to-all-start.1 = ((bf16[8,64,1792]{2,1,0:T(8,128)(2,1)}), bf16[8,64,1792]{2,1,0:T(8,128)(2,1)S(1)}, u32[]{:S(2)}, u32[]{:S(2)}) async-start(bf16[8,64,1792]{2,1,0:T(8,128)(2,1)} %bitcast.5), calls=%async_computation.1 | async-start | bytes 3670016 | tf_op jit(solution)/shard_map/all_to_all | solution.py:39
  105.6 54.1 %all-gather.2.cloned.1.call-start = ((), (), s32[]{:S(2)}) async-start(), calls=%async_computation.6 | async-start | bytes 2064384 | tf_op jit(solution)/shard_map/all_gather | solution.py:90
  127.9 0.9 copy-start.10
  129.9 4.2 %collective-permute-start = (bf16[64,896]{1,0:T(8,128)(2,1)S(1)}, bf16[64,896]{1,0:T(8,128)(2,1)S(1)}, u32[]{:S(2)}, u32[]{:S(2)}) collective-permute-start(bf16[64,896]{1,0:T(8,128)(2,1)S(1)} %get-tuple-element.16), channel_id=1, source_target_pairs={{0,32},{32,64},{64,96},{96,128},{128,160},{160,192},{192,224},{224... | collective-permute-start | bytes 344072 | tf_op jit(solution)/shard_map/ppermute | solution.py:79
  129.9 4.2 %collective-permute-start.1 = (bf16[64,896]{1,0:T(8,128)(2,1)S(1)}, bf16[64,896]{1,0:T(8,128)(2,1)S(1)}, u32[]{:S(2)}, u32[]{:S(2)}) collective-permute-start(bf16[64,896]{1,0:T(8,128)(2,1)S(1)} %get-tuple-element.16), channel_id=1, source_target_pairs={{0,224},{32,0},{64,32},{96,64},{128,96},{160,128},{192,160},{224,1... | collective-permute-start | bytes 344072 | tf_op jit(solution)/shard_map/ppermute | solution.py:82
  134.1 4.2 %collective-permute-start.2 = (bf16[64,896]{1,0:T(8,128)(2,1)S(1)}, bf16[64,896]{1,0:T(8,128)(2,1)S(1)}, u32[]{:S(2)}, u32[]{:S(2)}) collective-permute-start(bf16[64,896]{1,0:T(8,128)(2,1)S(1)} %collective-permute-done), channel_id=1, source_target_pairs={{0,32},{32,64},{64,96},{96,128},{128,160},{160,192},{192,224},{224... | collective-permute-start | bytes 344072 | tf_op jit(solution)/shard_map/ppermute | solution.py:79
  134.1 6.0 %collective-permute-start.3 = (bf16[64,896]{1,0:T(8,128)(2,1)S(1)}, bf16[64,896]{1,0:T(8,128)(2,1)S(1)}, u32[]{:S(2)}, u32[]{:S(2)}) collective-permute-start(bf16[64,896]{1,0:T(8,128)(2,1)S(1)} %collective-permute-done.1), channel_id=1, source_target_pairs={{0,224},{32,0},{64,32},{96,64},{128,96},{160,128},{192,160},{224,1... | collective-permute-start | bytes 344072 | tf_op jit(solution)/shard_map/ppermute | solution.py:82
  138.3 6.6 %collective-permute-start.4 = (bf16[64,896]{1,0:T(8,128)(2,1)S(1)}, bf16[64,896]{1,0:T(8,128)(2,1)S(1)}, u32[]{:S(2)}, u32[]{:S(2)}) collective-permute-start(bf16[64,896]{1,0:T(8,128)(2,1)S(1)} %collective-permute-done.2), channel_id=1, source_target_pairs={{0,32},{32,64},{64,96},{96,128},{128,160},{160,192},{192,224},{224... | collective-permute-start | bytes 344072 | tf_op jit(solution)/shard_map/ppermute | solution.py:79
  140.1 6.8 %collective-permute-start.5 = (bf16[64,896]{1,0:T(8,128)(2,1)S(1)}, bf16[64,896]{1,0:T(8,128)(2,1)S(1)}, u32[]{:S(2)}, u32[]{:S(2)}) collective-permute-start(bf16[64,896]{1,0:T(8,128)(2,1)S(1)} %collective-permute-done.3), channel_id=1, source_target_pairs={{0,224},{32,0},{64,32},{96,64},{128,96},{160,128},{192,160},{224,1... | collective-permute-start | bytes 344072 | tf_op jit(solution)/shard_map/ppermute | solution.py:82
  144.9 5.1 %collective-permute-start.6 = (bf16[64,896]{1,0:T(8,128)(2,1)S(1)}, bf16[64,896]{1,0:T(8,128)(2,1)S(1)}, u32[]{:S(2)}, u32[]{:S(2)}) collective-permute-start(bf16[64,896]{1,0:T(8,128)(2,1)S(1)} %collective-permute-done.4), channel_id=1, source_target_pairs={{0,32},{32,64},{64,96},{96,128},{128,160},{160,192},{192,224},{224... | collective-permute-start | bytes 344072 | tf_op jit(solution)/shard_map/ppermute | solution.py:79
  150.1 4.7 %copy-start = (bf16[512,896]{1,0:T(8,128)(2,1)}, bf16[512,896]{1,0:T(8,128)(2,1)S(1)}, u32[]{:S(2)}) copy-start(bf16[512,896]{1,0:T(8,128)(2,1)S(1)} %constant_dynamic-update-slice_fusion) | copy-start | bytes 2752516
  154.7 30.9 %all-to-all-start.2 = ((bf16[32,16,1024]{2,1,0:T(8,128)(2,1)}), bf16[32,16,1024]{2,1,0:T(8,128)(2,1)S(1)}, u32[]{:S(2)}, u32[]{:S(2)}) async-start(bf16[32,16,1024]{2,1,0:T(8,128)(2,1)} %bitcast.96), calls=%async_computation.2 | async-start | bytes 2097152 | tf_op jit(solution)/shard_map/all_to_all | solution.py:39
  159.8 3.8 %copy-start.4 = (bf16[1024,896]{0,1:T(8,128)(2,1)S(1)}, bf16[1024,896]{0,1:T(8,128)(2,1)}, u32[]{:S(2)}) copy-start(bf16[1024,896]{0,1:T(8,128)(2,1)} %copy.20) | copy-start | bytes 5505028
  159.8 3.8 %copy-start.7 = (bf16[8,128,7,128]{1,0,3,2:T(8,128)(2,1)S(1)}, bf16[8,128,7,128]{1,0,3,2:T(8,128)(2,1)}, u32[]{:S(2)}) copy-start(bf16[8,128,7,128]{1,0,3,2:T(8,128)(2,1)} %copy-done.6) | copy-start | bytes 5505028
  159.8 4.0 %copy-start.14 = (bf16[512,1792]{1,0:T(8,128)(2,1)S(1)}, bf16[512,1792]{1,0:T(8,128)(2,1)}, u32[]{:S(2)}) copy-start(bf16[512,1792]{1,0:T(8,128)(2,1)} %all-gather.2.cloned.1.call-done) | copy-start | bytes 5505028
  185.6 37.7 %all-to-all-start.5 = ((bf16[32,16,1024]{2,1,0:T(8,128)(2,1)}), bf16[32,16,1024]{2,1,0:T(8,128)(2,1)S(1)}, u32[]{:S(2)}, u32[]{:S(2)}) async-start(bf16[32,16,1024]{2,1,0:T(8,128)(2,1)} %bitcast.95), calls=%async_computation.5 | async-start | bytes 2097152 | tf_op jit(solution)/shard_map/all_to_all | solution.py:39
  194.3 1.2 copy-start.1
  199.1 1.5 copy-start.15
  208.4 1.5 copy-start.16
Sparse Core Ops, SparseCore 0:
  129.8 23.0 all-gather.1
